TPU v7x, 256 devices: a whole 4x4x8 slice. The times are simulated.
256 devices in a mesh: target: 32 (over x_lo, z, core), surface: 8 (over x_hi, y).
Axes of the slice: x: 4 (x_hi: 2, x_lo: 2; x = x_hi * 2 + x_lo), y: 4, z: 8, core: 2. Of those that a mesh axis runs over, the one named last changes fastest.
Arguments:
- response: float32 [64, 32, 32, 512], P('target', None, 'surface'), may hold values from -6 to 6
- data_spectra: bfloat16 [32, 16, 2, 32, 32, 256], P('target', None, None, 'surface'), may hold values from -0.01171875 to 0.01171875
- observed: bfloat16 [32, 2, 32, 32, 256], P('target', None, None, 'surface'), may hold values from -6 to 6
- block_lists: int32 [32, 16], replicated, may hold values from 0 to 63, as said below
Outputs:
- response_next: float32 [64, 32, 32, 512], P('target', None, 'surface')
- response_copy: bfloat16 [64, 32, 32, 512], P('target', None, 'surface')
- residual: float32 [32, 2, 32, 32, 256], P('target', None, None, 'surface')
Inputs may be any that keep to these rules, and one draw needn't show every extreme that they name: `block_lists`: block b is owned by index b // 2 of target. Each tile lists 16 blocks, no two of the same owner.
All inputs are finite; a program needn't handle non-finite values.
Results may differ from a plain program's by a relative error of at most 0.0048.
Values may be sent and summed in bfloat16 or wider, within the bound.
No kernel may reach another device: no remote copies, remote signals or barrier semaphores. Data moves between devices by JAX's collectives and lax.ppermute only.
A program may use at most 128 MiB of HBM per device.

v0:
```python
import math

import jax
import jax.numpy as jnp
from jax import lax
from jax.sharding import PartitionSpec as P

step_length = 0.5


def make_table(samples):
    freqs = samples // 2
    sample_index = lax.broadcasted_iota(jnp.int32, (samples, freqs), 0)
    freq_index = lax.broadcasted_iota(jnp.int32, (samples, freqs), 1)
    phase = (sample_index * freq_index % samples).astype(jnp.float32) * (2.0 * math.pi / samples)
    return jnp.concatenate([jnp.cos(phase), -jnp.sin(phase)], axis=1)


def contract(spec, listed):
    return jnp.einsum("lakf,lkrf->arf", spec, listed, preferred_element_type=jnp.float32)


def correlate(misfit_part, listed):
    return jnp.einsum("arf,lkrf->lakf", misfit_part, listed, preferred_element_type=jnp.float32)


def per_device(response, data_spectra, observed, block_lists):
    owners = lax.axis_size("target")
    my_index = lax.axis_index("target")
    owned = response.shape[0]
    samples = response.shape[3]
    freqs = samples // 2
    dft_table = make_table(samples)
    table_half = dft_table.astype(jnp.bfloat16)
    own_ids = lax.dynamic_slice_in_dim(block_lists, my_index, 1, 0)[0]
    own_owner = own_ids // owned
    wanted = block_lists // owned == my_index
    present = jnp.any(wanted, axis=1)
    slot_for = jnp.sum(jnp.where(wanted, block_lists % owned, 0), axis=1)
    picker = (
        (slot_for[None, :] == jnp.arange(owned, dtype=jnp.int32)[:, None]) & present[None, :]
    ).astype(jnp.float32)
    present_rows = present[:, None, None, None]
    zero_half = jnp.zeros((), jnp.bfloat16)
    copy_now = response.astype(jnp.bfloat16)
    outgoing = jnp.where(present_rows, copy_now[slot_for], zero_half)
    arrived = lax.all_to_all(outgoing, "target", split_axis=0, concat_axis=0, tiled=True)
    spectra = jnp.dot(arrived[own_owner], table_half, preferred_element_type=jnp.float32).astype(
        jnp.bfloat16
    )
    listed_data = data_spectra[0]
    spec_real = spectra[..., :freqs]
    spec_imag = spectra[..., freqs:]
    data_real = listed_data[:, 0]
    data_imag = listed_data[:, 1]
    partial_value = jnp.stack(
        [
            contract(spec_real, data_real) - contract(spec_imag, data_imag),
            contract(spec_real, data_imag) + contract(spec_imag, data_real),
        ]
    )
    observed_share = observed[0].astype(jnp.float32)
    summed_share = lax.psum_scatter(partial_value, "surface", scatter_dimension=2, tiled=True)
    residual_share = observed_share - summed_share
    misfit = lax.all_gather(residual_share.astype(jnp.bfloat16), "surface", axis=2, tiled=True)
    misfit_real = misfit[0]
    misfit_imag = misfit[1]
    grad_spectra = jnp.concatenate(
        [
            -(correlate(misfit_real, data_real) + correlate(misfit_imag, data_imag)),
            correlate(misfit_real, data_imag) - correlate(misfit_imag, data_real),
        ],
        axis=-1,
    )
    grad_time = jnp.dot(grad_spectra, dft_table.T, precision=lax.Precision.HIGHEST)
    returning = jnp.zeros((owners,) + grad_time.shape[1:], jnp.float32).at[own_owner].set(grad_time)
    received = lax.all_to_all(returning, "target", split_axis=0, concat_axis=0, tiled=True)
    flat = received.reshape(owners, -1)
    gradient = jnp.dot(picker, flat, precision=lax.Precision.HIGHEST).reshape(response.shape)
    response_next = response - step_length * gradient
    return (response_next, response_next.astype(jnp.bfloat16), residual_share[None])


def solution(mesh):
    return jax.shard_map(
        per_device,
        mesh=mesh,
        in_specs=(
            P("target", None, "surface", None),
            P("target", None, None, "surface", None, None),
            P("target", None, None, "surface", None),
            P(),
        ),
        out_specs=(
            P("target", None, "surface", None),
            P("target", None, "surface", None),
            P("target", None, None, "surface", None),
        ),
        check_vma=False,
    )
```

profile of v0, /device:TPU:1, one launch (start us, length us, event | category | flops | bytes accessed | tf_op | source)
XLA Modules:
  0.0 649.7 jit_solution(16325674682704119219)
XLA Ops:
  7.2 0.7 fusion.57
  7.9 0.7 fusion.44
  8.6 1.1 convert_element_type.29
  9.8 5.7 gather_fusion
  15.5 5.9 broadcast_select_fusion
  21.3 0.0 copy-start.4
  21.4 11.2 %all-to-all-start = ((bf16[32,32,4,512]{3,2,1,0:T(4,128)(2,1)}), bf16[32,32,4,512]{3,2,1,0:T(4,128)(2,1)}, u32[]{:S(2)}, u32[]{:S(2)}) async-start(bf16[32,32,4,512]{3,2,1,0:T(4,128)(2,1)} %broadcast_select_fusion), calls=%async_computation | async-start | bytes 8388608 | tf_op jit(solution)/shard_map/all_to_all | solution.py:47
  32.6 0.3 reduce-scatter.2.cloned.1.call-start
  32.8 0.0 copy-done.4
  32.8 0.0 copy-start.7
  32.9 12.0 %copy.72 = bf16[1,16,2,4,32,256]{4,1,3,5,2,0:T(8,128)(2,1)} copy(bf16[1,16,2,4,32,256]{5,4,3,2,1,0:T(8,128)(2,1)S(1)} %copy-done.4) | data formatting | bytes 4194304 | tf_op args[1]
  44.9 0.0 copy-done.7
  44.9 0.2 dynamic-slice_reduce_fusion
  45.1 2.1 sine_negate_fusion
  47.2 80.1 %all-to-all-done = bf16[32,32,4,512]{3,2,1,0:T(4,128)(2,1)} async-done(((bf16[32,32,4,512]{3,2,1,0:T(4,128)(2,1)}), bf16[32,32,4,512]{3,2,1,0:T(4,128)(2,1)}, u32[]{:S(2)}, u32[]{:S(2)}) %all-to-all-start) | async-done | bytes 4194336 | tf_op jit(solution)/shard_map/all_to_all | solution.py:47
  127.2 4.5 gather_fusion.1
  131.8 1.3 fusion.20
  133.0 0.3 fusion.59
  133.3 6.5 %copy.73 = bf16[16,32,4,256]{1,0,2,3:T(8,128)(2,1)} copy(bf16[16,32,4,256]{3,1,2,0:T(8,128)(2,1)S(1)} %get-tuple-element.20) | data formatting | bytes 2097152 | tf_op jit(solution)/shard_map/slice | solution.py:52
  139.8 6.7 %copy.74 = bf16[16,32,4,256]{1,0,2,3:T(8,128)(2,1)} copy(bf16[16,32,4,256]{3,1,2,0:T(8,128)(2,1)S(1)} %get-tuple-element.21) | data formatting | bytes 2097152 | tf_op jit(solution)/shard_map/slice | solution.py:53
  146.6 0.0 copy-start
  146.6 0.0 slice-start
  146.6 6.9 %fusion.9 = f32[256,32,32,1]{2,1,3,0:T(8,128)} fusion(bf16[16,32,4,256]{1,0,2,3:T(8,128)(2,1)} %copy.74, bf16[16,2,4,32,256]{3,0,2,4,1:T(8,128)(2,1)} %bitcast.108), kind=kOutput, calls=%fused_computation.20 | convolution fusion | flops 33554432 | bytes 9437184 | tf_op jit(solution)/shard_map/lakf,lkrf->arf/dot_general | solution.py:20
  153.5 0.0 copy-done
  153.5 3.7 fusion.10
  157.2 0.0 slice-done
  157.2 0.0 slice-done.1
  157.2 0.0 copy-start.1
  157.2 5.7 fusion.6
  162.9 0.0 copy-done.1
  162.9 3.2 fusion.7
  166.2 0.0 copy-done.2
  166.2 6.5 pad_maximum_fusion
  172.6 8.0 %copy.77 = f32[2,32,32,256]{3,1,0,2:T(8,128)} copy(f32[2,32,32,256]{2,1,3,0:T(8,128)} %pad_maximum_fusion) | data formatting | bytes 4194304 | tf_op jit(solution)/shard_map/stack | solution.py:56
  180.6 0.0 reduce-scatter.2.cloned.1.call-update
  180.6 0.0 all-gather.2.cloned.1.call-start
  180.7 78.7 %reduce-scatter.2.cloned.1.call-done = f32[2,32,4,256]{3,1,0,2:T(8,128)} async-done(((f32[2,32,32,256]{3,1,0,2:T(8,128)}), f32[2,32,4,256]{3,1,0,2:T(8,128)}) %reduce-scatter.2.cloned.1.call-update) | async-done | bytes 262160 | tf_op jit(solution)/shard_map/reduce_scatter | solution.py:63
  259.3 0.0 copy-done.6
  259.3 1.6 fusion.40
  261.0 0.0 all-gather.2.cloned.1.call-update
  261.0 51.8 %all-gather.2.cloned.1.call-done = bf16[2,32,32,256]{3,1,0,2:T(8,128)(2,1)} async-done(((bf16[2,32,4,256]{3,1,0,2:T(8,128)(2,1)}), bf16[2,32,32,256]{3,1,0,2:T(8,128)(2,1)}) %all-gather.2.cloned.1.call-update) | async-done | bytes 1048592 | tf_op jit(solution)/shard_map/all_gather | solution.py:65
  312.8 2.2 fusion.60
  315.1 14.5 %copy.97 = bf16[1,32,32,256]{2,1,3,0:T(8,128)(2,1)S(1)} copy(bf16[1,32,32,256]{3,1,0,2:T(8,128)(2,1)} %get-tuple-element.23) | data formatting | bytes 1048576
  329.6 6.6 %fusion.11 = f32[256,32,16,4]{1,2,3,0:T(8,128)} fusion(bf16[16,2,4,32,256]{3,0,2,4,1:T(8,128)(2,1)} %bitcast.110, bf16[1,32,32,256]{2,1,3,0:T(8,128)(2,1)S(1)} %copy.97), kind=kOutput, calls=%fused_computation.22 | convolution fusion | flops 33554432 | bytes 6815744 | tf_op jit(solution)/shard_map/arf,lkrf->lakf/dot_general | solution.py:24
  336.3 6.7 %fusion.8 = f32[256,32,16,4]{1,2,3,0:T(8,128)} fusion(bf16[16,2,4,32,256]{3,0,2,4,1:T(8,128)(2,1)} %bitcast.111, bf16[1,32,32,256]{2,1,3,0:T(8,128)(2,1)S(1)} %copy.97), kind=kOutput, calls=%fused_computation.19 | convolution fusion | flops 33554432 | bytes 6815744 | tf_op jit(solution)/shard_map/arf,lkrf->lakf/dot_general | solution.py:24
  342.9 4.5 copy.98
  347.4 9.1 %subtract_bitcast_fusion = f32[16,32,4,256]{1,0,2,3:T(8,128)} fusion(f32[256,32,16,4]{1,2,3,0:T(8,128)} %fusion.11, bf16[16,2,4,32,256]{3,0,2,4,1:T(8,128)(2,1)} %bitcast.112, bf16[1,32,32,256]{2,1,3,0:T(8,128)(2,1)S(1)} %copy.98), kind=kOutput, calls=%fused_computation.6 | convolution fusion | flops 34078720 | bytes 15204352 | tf_op jit(solution)/shard_map/arf,lkrf->lakf/dot_general | solution.py:24
  356.5 7.4 %copy.81 = f32[16,32,4,256]{3,1,2,0:T(8,128)} copy(f32[16,32,4,256]{1,0,2,3:T(8,128)} %subtract_bitcast_fusion) | data formatting | bytes 4194304 | tf_op jit(solution)/shard_map/sub | solution.py:71
  363.9 9.1 %negate_bitcast_fusion = f32[16,32,4,256]{1,0,2,3:T(8,128)} fusion(f32[256,32,16,4]{1,2,3,0:T(8,128)} %fusion.8, bf16[16,2,4,32,256]{3,0,2,4,1:T(8,128)(2,1)} %bitcast.113, bf16[1,32,32,256]{2,1,3,0:T(8,128)(2,1)S(1)} %copy.98), kind=kOutput, calls=%fused_computation.7 | convolution fusion | flops 34603008 | bytes 15204352 | tf_op jit(solution)/shard_map/arf,lkrf->lakf/dot_general | solution.py:24
  373.0 7.6 %copy.80 = f32[16,32,4,256]{3,1,2,0:T(8,128)} copy(f32[16,32,4,256]{1,0,2,3:T(8,128)} %negate_bitcast_fusion) | data formatting | bytes 4194304 | tf_op jit(solution)/shard_map/neg | solution.py:70
  380.6 0.0 copy-done.3
  380.6 9.6 %fusion.2 = f32[16,32,4,512]{3,1,2,0:T(8,128)} fusion(f32[16,32,4,256]{3,1,2,0:T(8,128)S(1)} %copy-done.3, f32[16,32,4,256]{3,1,2,0:T(8,128)} %copy.80, f32[512,256]{1,0:T(8,128)S(1)} %get-tuple-element.28, f32[512,256]{1,0:T(8,128)S(1)} %get-tuple-element.29), kind=kOutput, calls=%fused_computation.10 | convolution fusion | flops 6443761664 | bytes 9437184 | tf_op jit(solution)/shard_map/dot_general | solution.py:75
  390.3 4.3 broadcast_in_dim.18
  394.6 8.0 %scatter_fusion = f32[32,32,4,512]{3,1,2,0:T(8,128)} fusion(f32[32,32,4,512]{3,1,2,0:T(8,128)} %broadcast_in_dim.18, s32[16]{0:T(128)S(1)} %fusion.52, f32[16,32,4,512]{3,1,2,0:T(8,128)} %fusion.2), kind=kCustom, calls=%fused_computation.2 | custom fusion | bytes 12582976 | tf_op jit(solution)/shard_map/scatter | solution.py:76
  402.6 9.8 %all-to-all-start.1 = ((f32[32,32,4,512]{3,1,2,0:T(8,128)}), f32[32,32,4,512]{3,1,2,0:T(8,128)}, u32[]{:S(2)}, u32[]{:S(2)}) async-start(f32[32,32,4,512]{3,1,2,0:T(8,128)} %scatter_fusion), calls=%async_computation.2 | async-start | bytes 16777216 | tf_op jit(solution)/shard_map/all_to_all | solution.py:77
  412.3 0.9 copy.87
  413.2 183.0 %all-to-all-done.1 = f32[32,32,4,512]{3,1,2,0:T(8,128)} async-done(((f32[32,32,4,512]{3,1,2,0:T(8,128)}), f32[32,32,4,512]{3,1,2,0:T(8,128)}, u32[]{:S(2)}, u32[]{:S(2)}) %all-to-all-start.1) | async-done | bytes 8388640 | tf_op jit(solution)/shard_map/all_to_all | solution.py:77
  596.3 13.8 %copy.82 = f32[32,32,4,512]{3,2,1,0:T(4,128)} copy(f32[32,32,4,512]{3,1,2,0:T(8,128)} %all-to-all-done.1) | data formatting | bytes 16777216 | tf_op jit(solution)/shard_map/all_to_all | solution.py:77
  610.0 9.8 %reshape.108 = f32[32,65536]{1,0:T(8,128)} reshape(f32[32,32,4,512]{3,2,1,0:T(4,128)} %copy.82) | data formatting | bytes 16777216 | tf_op jit(solution)/shard_map/reshape | solution.py:78
  619.8 10.0 %dot_general.48 = f32[32,4,512,32]{2,1,0,3:T(4,128)} reshape(f32[65536,32]{0,1:T(8,128)} %bitcast.118) | data formatting | bytes 16777216 | tf_op jit(solution)/shard_map/dot_general | solution.py:79
  629.8 0.0 copy-done.5
  629.8 10.8 %fusion.61 = (bf16[2,32,4,512]{3,0,2,1:T(2,128)(2,1)S(1)}, f32[2,32,4,512]{3,0,2,1:T(2,128)S(1)}) fusion(f32[32,4,512,32]{2,1,0,3:T(4,128)} %dot_general.48, pred[32]{0:T(512)(128)(4,1)S(1)} %get-tuple-element.18, s32[32]{0:T(128)S(1)} %fusion.44, f32[2,32,4,512]{3,2,1,0:T(4,128)S(1)} %copy-done.5), kind=kOutput, calls=%fused_computation.86 | convolution fusion | flops 50724992 | bytes 9699488 | tf_op jit(solution)/shard_map/dot_general | solution.py:79
  640.7 0.8 copy.86
  641.5 0.9 copy.85
  (10 shorter events, 0.0 us)
Async XLA Ops:
  21.3 11.5 %copy-start.4 = (bf16[1,16,2,4,32,256]{5,4,3,2,1,0:T(8,128)(2,1)S(1)}, bf16[1,16,2,4,32,256]{5,4,3,2,1,0:T(8,128)(2,1)}, u32[]{:S(2)}) copy-start(bf16[1,16,2,4,32,256]{5,4,3,2,1,0:T(8,128)(2,1)} %param.5) | copy-start | bytes 6291460
  21.4 105.9 %all-to-all-start = ((bf16[32,32,4,512]{3,2,1,0:T(4,128)(2,1)}), bf16[32,32,4,512]{3,2,1,0:T(4,128)(2,1)}, u32[]{:S(2)}, u32[]{:S(2)}) async-start(bf16[32,32,4,512]{3,2,1,0:T(4,128)(2,1)} %broadcast_select_fusion), calls=%async_computation | async-start | bytes 8388608 | tf_op jit(solution)/shard_map/all_to_all | solution.py:47
  32.6 226.8 %reduce-scatter.2.cloned.1.call-start = ((), (), s32[]{:S(2)}) async-start(), calls=%async_computation.3 | async-start | bytes 2359296 | tf_op jit(solution)/shard_map/reduce_scatter | solution.py:63
  32.8 12.0 %copy-start.7 = (s32[32,16]{0,1:T(8,128)S(1)}, s32[32,16]{0,1:T(8,128)}, u32[]{:S(2)}) copy-start(s32[32,16]{0,1:T(8,128)} %param.7) | copy-start | bytes 6148
  146.6 6.9 %copy-start = (bf16[16,32,4,256]{1,0,2,3:T(8,128)(2,1)S(1)}, bf16[16,32,4,256]{1,0,2,3:T(8,128)(2,1)}, u32[]{:S(2)}) copy-start(bf16[16,32,4,256]{1,0,2,3:T(8,128)(2,1)} %copy.73) | copy-start | bytes 3145732
  146.6 10.6 %slice-start = ((s8[8388608]{0:T(1024)(128)(4,1)}), s8[4194304]{0:T(1024)(128)(4,1)S(1)}, s32[]{:S(2)}) async-start(s8[8388608]{0:T(1024)(128)(4,1)} %bitcast.114), calls=%async_computation.5 | async-start | bytes 8388608
  153.5 3.7 slice-start.1
  157.2 5.7 copy-start.1
  162.9 3.2 copy-start.2
  172.6 86.7 %copy-start.6 = (bf16[1,2,32,4,256]{4,3,2,1,0:T(4,128)(2,1)S(1)}, bf16[1,2,32,4,256]{4,3,2,1,0:T(4,128)(2,1)}, u32[]{:S(2)}) copy-start(bf16[1,2,32,4,256]{4,3,2,1,0:T(4,128)(2,1)} %param.6) | copy-start | bytes 393220
  180.6 132.2 %all-gather.2.cloned.1.call-start = ((), (), s32[]{:S(2)}) async-start(), calls=%async_computation.4 | async-start | bytes 1179648 | tf_op jit(solution)/shard_map/all_gather | solution.py:65
  373.0 7.6 %copy-start.3 = (f32[16,32,4,256]{3,1,2,0:T(8,128)S(1)}, f32[16,32,4,256]{3,1,2,0:T(8,128)}, u32[]{:S(2)}) copy-start(f32[16,32,4,256]{3,1,2,0:T(8,128)} %copy.81) | copy-start | bytes 6291460
  402.6 193.7 %all-to-all-start.1 = ((f32[32,32,4,512]{3,1,2,0:T(8,128)}), f32[32,32,4,512]{3,1,2,0:T(8,128)}, u32[]{:S(2)}, u32[]{:S(2)}) async-start(f32[32,32,4,512]{3,1,2,0:T(8,128)} %scatter_fusion), calls=%async_computation.2 | async-start | bytes 16777216 | tf_op jit(solution)/shard_map/all_to_all | solution.py:77
  619.8 10.0 %copy-start.5 = (f32[2,32,4,512]{3,2,1,0:T(4,128)S(1)}, f32[2,32,4,512]{3,2,1,0:T(4,128)}, u32[]{:S(2)}) copy-start(f32[2,32,4,512]{3,2,1,0:T(4,128)} %param.4) | copy-start | bytes 1572868
Sparse Core Ops, SparseCore 0:
  180.7 78.5 reduce-scatter.1
  262.6 50.2 all-gather.1
where the time goes:
time: 656 us; the launch traced here: 650 us
  waiting for transfers between devices  394 us (60%)
  local copies, waits for them, and re-layouts  129 us (20%)
  matrix products  72.7 us (11%)
  starting transfers between devices  21.3 us (3%)
  other arithmetic  18.7 us (3%)
  between operations  14.7 us (2%)
    all_to_all x1, waiting for transfers between devices, per_device(): lax.all_to_all(returning, 'target', split_axis=0, concat_axis=0, tiled=True)  183 us
    all_to_all x1, waiting for transfers between devices, per_device(): lax.all_to_all(outgoing, 'target', split_axis=0, concat_axis=0, tiled=True)  80.1 us
    reduce_scatter x1, waiting for transfers between devices, per_device(): lax.psum_scatter(partial_value, 'surface', scatter_dimension=2, tiled=True)  78.7 us
    all_gather x1, waiting for transfers between devices, per_device(): lax.all_gather(residual_share.astype(jnp.bfloat16), 'surface', axis=2, ti...  51.8 us
    unnamed x26, local copies, waits for them, and re-layouts  33.6 us
    dot_general x4, matrix products, correlate(): jnp.einsum('arf,lkrf->lakf', misfit_part, listed, preferred_element_type=...  31.6 us
    dot_general x4, matrix products, contract(): jnp.einsum('lakf,lkrf->arf', spec, listed, preferred_element_type=jnp.flo...  19.5 us
    all_to_all x1, local copies, waits for them, and re-layouts, per_device(): lax.all_to_all(returning, 'target', split_axis=0, concat_axis=0, tiled=True)  13.8 us
  transfers between devices with their start and end apart: 4, of which 4 were waited for; matrix products, arithmetic and copies ran while one was open for 2% of the time, Pallas kernels for 0%

commit v1 on v0

--- a/solution.py
+++ b/solution.py
@@ -73,10 +73,13 @@
         axis=-1,
     )
     grad_time = jnp.dot(grad_spectra, dft_table.T, precision=lax.Precision.HIGHEST)
-    returning = jnp.zeros((owners,) + grad_time.shape[1:], jnp.float32).at[own_owner].set(grad_time)
+    grad_half = grad_time.astype(jnp.bfloat16)
+    returning = jnp.zeros((owners,) + grad_time.shape[1:], jnp.bfloat16).at[own_owner].set(grad_half)
     received = lax.all_to_all(returning, "target", split_axis=0, concat_axis=0, tiled=True)
     flat = received.reshape(owners, -1)
-    gradient = jnp.dot(picker, flat, precision=lax.Precision.HIGHEST).reshape(response.shape)
+    gradient = jnp.dot(
+        picker.astype(jnp.bfloat16), flat, preferred_element_type=jnp.float32
+    ).reshape(response.shape)
     response_next = response - step_length * gradient
     return (response_next, response_next.astype(jnp.bfloat16), residual_share[None])
 

time: 656 us -> 528 us (0.80)
  waiting for transfers between devices: 394 us -> 305 us
  local copies, waits for them, and re-layouts: 129 us -> 98 us
    all_to_all x1, waiting for transfers between devices: 183 us -> 93.8 us  [per_device(): lax.all_to_all(returning, 'target', split_axis=0, concat_axis=0, tiled=True)]
    unnamed x26 -> x29, local copies, waits for them, and re-layouts: 33.6 us -> 25 us
  transfers between devices with their start and end apart: 4 -> 4, of which waited for: 4 -> 4; matrix products, arithmetic and copies ran while one was open for 2% -> 3% of each run, Pallas kernels for 0% -> 0%
where the time goes in v1:
time: 528 us; the launch traced here: 521 us
  waiting for transfers between devices  305 us (58%)
  local copies, waits for them, and re-layouts  98 us (19%)
  matrix products  66.7 us (13%)
  starting transfers between devices  20.7 us (4%)
  other arithmetic  16.1 us (3%)
  between operations  14.6 us (3%)
    all_to_all x1, waiting for transfers between devices, per_device(): lax.all_to_all(returning, 'target', split_axis=0, concat_axis=0, tiled=True)  93.8 us
    all_to_all x1, waiting for transfers between devices, per_device(): lax.all_to_all(outgoing, 'target', split_axis=0, concat_axis=0, tiled=True)  80.3 us
    reduce_scatter x1, waiting for transfers between devices, per_device(): lax.psum_scatter(partial_value, 'surface', scatter_dimension=2, tiled=True)  78.6 us
    all_gather x1, waiting for transfers between devices, per_device(): lax.all_gather(residual_share.astype(jnp.bfloat16), 'surface', axis=2, ti...  51.8 us
    dot_general x4, matrix products, correlate(): jnp.einsum('arf,lkrf->lakf', misfit_part, listed, preferred_element_type=...  31.5 us
    unnamed x29, local copies, waits for them, and re-layouts  25 us
    dot_general x4, matrix products, contract(): jnp.einsum('lakf,lkrf->arf', spec, listed, preferred_element_type=jnp.flo...  19.5 us
    all_to_all x1, starting transfers between devices, per_device(): lax.all_to_all(outgoing, 'target', split_axis=0, concat_axis=0, tiled=True)  11.2 us
  transfers between devices with their start and end apart: 4, of which 4 were waited for; matrix products, arithmetic and copies ran while one was open for 3% of the time, Pallas kernels for 0%

profile of v1, /device:TPU:1, one launch (start us, length us, event | category | flops | bytes accessed | tf_op | source)
XLA Modules:
  0.0 520.8 jit_solution(17494378775718084115)
XLA Ops:
  7.2 0.7 fusion.53
  7.9 0.7 fusion.42
  8.6 1.2 copy.108
  9.8 2.7 gather_fusion
  12.6 4.5 broadcast_select_fusion
  17.0 11.2 %all-to-all-start = ((bf16[32,32,4,512]{3,1,2,0:T(8,128)(2,1)}), bf16[32,32,4,512]{3,1,2,0:T(8,128)(2,1)}, u32[]{:S(2)}, u32[]{:S(2)}) async-start(bf16[32,32,4,512]{3,1,2,0:T(8,128)(2,1)} %broadcast_select_fusion), calls=%async_computation | async-start | bytes 8388608 | tf_op jit(solution)/shard_map/all_to_all | solution.py:47
  28.3 0.0 reduce-scatter.2.cloned.1.call-start
  28.3 0.0 copy-done.5
  28.3 0.0 copy-start.8
  28.3 12.0 %copy.71 = bf16[1,16,2,4,32,256]{4,1,3,5,2,0:T(8,128)(2,1)} copy(bf16[1,16,2,4,32,256]{5,4,3,2,1,0:T(8,128)(2,1)S(1)} %copy-done.5) | data formatting | bytes 4194304 | tf_op args[1]
  40.4 0.0 copy-done.8
  40.4 0.2 dynamic-slice_reduce_fusion
  40.6 2.1 sine_negate_fusion
  42.6 80.3 %all-to-all-done = bf16[32,32,4,512]{3,1,2,0:T(8,128)(2,1)} async-done(((bf16[32,32,4,512]{3,1,2,0:T(8,128)(2,1)}), bf16[32,32,4,512]{3,1,2,0:T(8,128)(2,1)}, u32[]{:S(2)}, u32[]{:S(2)}) %all-to-all-start) | async-done | bytes 4194336 | tf_op jit(solution)/shard_map/all_to_all | solution.py:47
  122.9 2.9 gather_fusion.1
  125.8 1.3 convolution_convert_fusion
  127.1 0.3 fusion.55
  127.3 6.4 %copy.72 = bf16[16,32,4,256]{1,0,2,3:T(8,128)(2,1)} copy(bf16[16,32,4,256]{3,1,2,0:T(8,128)(2,1)S(1)} %get-tuple-element.20) | data formatting | bytes 2097152 | tf_op jit(solution)/shard_map/slice | solution.py:52
  133.8 6.6 %copy.73 = bf16[16,32,4,256]{1,0,2,3:T(8,128)(2,1)} copy(bf16[16,32,4,256]{3,1,2,0:T(8,128)(2,1)S(1)} %get-tuple-element.21) | data formatting | bytes 2097152 | tf_op jit(solution)/shard_map/slice | solution.py:53
  140.4 0.0 copy-start.1
  140.5 0.0 slice-start
  140.5 6.9 %fusion.10 = f32[256,32,32,1]{2,1,3,0:T(8,128)} fusion(bf16[16,32,4,256]{1,0,2,3:T(8,128)(2,1)} %copy.72, bf16[16,2,4,32,256]{3,0,2,4,1:T(8,128)(2,1)} %bitcast.108), kind=kOutput, calls=%fused_computation.21 | convolution fusion | flops 33554432 | bytes 9437184 | tf_op jit(solution)/shard_map/lakf,lkrf->arf/dot_general | solution.py:20
  147.3 0.0 copy-done.1
  147.3 3.7 fusion.9
  151.0 0.0 slice-done
  151.0 0.0 slice-done.1
  151.1 0.0 copy-start
  151.1 5.7 %fusion.5 = f32[1,32,32,256]{2,1,3,0:T(8,128)} fusion(f32[256,32,32,1]{2,1,3,0:T(8,128)} %fusion.10, bf16[16,32,4,256]{1,0,2,3:T(8,128)(2,1)S(1)} %copy-done.1, bf16[16,2,4,32,256]{3,0,2,4,1:T(8,128)(2,1)S(1)} %bitcast.116), kind=kOutput, calls=%fused_computation.15 | convolution fusion | flops 33816576 | bytes 10485760 | tf_op jit(solution)/shard_map/lakf,lkrf->arf/dot_general | solution.py:20
  156.8 0.0 copy-done
  156.8 3.2 fusion.4
  160.0 0.0 copy-done.2
  160.0 6.5 %pad_maximum_fusion = f32[2,32,32,256]{2,1,3,0:T(8,128)} fusion(f32[1,32,32,256]{2,1,3,0:T(8,128)} %fusion.4, f32[1,32,32,256]{2,1,3,0:T(8,128)S(1)} %copy-done.2), kind=kLoop, calls=%fused_computation.3 | loop fusion | flops 524288 | bytes 4194304 | tf_op jit(solution)/shard_map/stack | solution.py:56
  166.5 7.9 %copy.76 = f32[2,32,32,256]{3,1,0,2:T(8,128)} copy(f32[2,32,32,256]{2,1,3,0:T(8,128)} %pad_maximum_fusion) | data formatting | bytes 4194304 | tf_op jit(solution)/shard_map/stack | solution.py:56
  174.4 0.0 reduce-scatter.2.cloned.1.call-update
  174.5 0.0 all-gather.2.cloned.1.call-start
  174.5 78.6 %reduce-scatter.2.cloned.1.call-done = f32[2,32,4,256]{3,1,0,2:T(8,128)} async-done(((f32[2,32,32,256]{3,1,0,2:T(8,128)}), f32[2,32,4,256]{3,1,0,2:T(8,128)}) %reduce-scatter.2.cloned.1.call-update) | async-done | bytes 262160 | tf_op jit(solution)/shard_map/reduce_scatter | solution.py:63
  253.1 0.0 copy-done.7
  253.2 1.6 fusion.38
  254.8 0.0 all-gather.2.cloned.1.call-update
  254.8 51.8 %all-gather.2.cloned.1.call-done = bf16[2,32,32,256]{3,1,0,2:T(8,128)(2,1)} async-done(((bf16[2,32,4,256]{3,1,0,2:T(8,128)(2,1)}), bf16[2,32,32,256]{3,1,0,2:T(8,128)(2,1)}) %all-gather.2.cloned.1.call-update) | async-done | bytes 1048592 | tf_op jit(solution)/shard_map/all_gather | solution.py:65
  306.6 2.2 fusion.56
  308.9 4.6 copy.96
  313.5 6.6 %fusion.8 = f32[256,32,16,4]{1,2,3,0:T(8,128)} fusion(bf16[16,2,4,32,256]{3,0,2,4,1:T(8,128)(2,1)} %bitcast.110, bf16[1,32,32,256]{2,1,3,0:T(8,128)(2,1)S(1)} %copy.96), kind=kOutput, calls=%fused_computation.19 | convolution fusion | flops 33554432 | bytes 6815744 | tf_op jit(solution)/shard_map/arf,lkrf->lakf/dot_general | solution.py:24
  320.2 6.7 %fusion.11 = f32[256,32,16,4]{1,2,3,0:T(8,128)} fusion(bf16[16,2,4,32,256]{3,0,2,4,1:T(8,128)(2,1)} %bitcast.111, bf16[1,32,32,256]{2,1,3,0:T(8,128)(2,1)S(1)} %copy.96), kind=kOutput, calls=%fused_computation.22 | convolution fusion | flops 33554432 | bytes 6815744 | tf_op jit(solution)/shard_map/arf,lkrf->lakf/dot_general | solution.py:24
  326.8 4.5 copy.97
  331.3 9.1 %negate_bitcast_fusion = f32[16,32,4,256]{1,0,2,3:T(8,128)} fusion(f32[256,32,16,4]{1,2,3,0:T(8,128)} %fusion.8, bf16[16,2,4,32,256]{3,0,2,4,1:T(8,128)(2,1)} %bitcast.112, bf16[1,32,32,256]{2,1,3,0:T(8,128)(2,1)S(1)} %copy.97), kind=kOutput, calls=%fused_computation.5 | convolution fusion | flops 34603008 | bytes 15204352 | tf_op jit(solution)/shard_map/arf,lkrf->lakf/dot_general | solution.py:24
  340.4 7.4 %copy.79 = f32[16,32,4,256]{3,1,2,0:T(8,128)} copy(f32[16,32,4,256]{1,0,2,3:T(8,128)} %negate_bitcast_fusion) | data formatting | bytes 4194304 | tf_op jit(solution)/shard_map/neg | solution.py:70
  347.8 9.1 %subtract_bitcast_fusion = f32[16,32,4,256]{1,0,2,3:T(8,128)} fusion(f32[256,32,16,4]{1,2,3,0:T(8,128)} %fusion.11, bf16[16,2,4,32,256]{3,0,2,4,1:T(8,128)(2,1)} %bitcast.113, bf16[1,32,32,256]{2,1,3,0:T(8,128)(2,1)S(1)} %copy.97), kind=kOutput, calls=%fused_computation.4 | convolution fusion | flops 34078720 | bytes 15204352 | tf_op jit(solution)/shard_map/arf,lkrf->lakf/dot_general | solution.py:24
  356.9 7.6 %copy.80 = f32[16,32,4,256]{3,1,2,0:T(8,128)} copy(f32[16,32,4,256]{1,0,2,3:T(8,128)} %subtract_bitcast_fusion) | data formatting | bytes 4194304 | tf_op jit(solution)/shard_map/sub | solution.py:71
  364.5 0.0 copy-done.3
  364.5 9.5 %fusion.18 = bf16[16,32,4,512]{3,1,2,0:T(8,128)(2,1)} fusion(f32[16,32,4,256]{3,1,2,0:T(8,128)} %copy.80, f32[16,32,4,256]{3,1,2,0:T(8,128)S(1)} %copy-done.3, f32[512,256]{1,0:T(8,128)S(1)} %get-tuple-element.28, f32[512,256]{1,0:T(8,128)S(1)} %get-tuple-element.29), kind=kOutput, calls=%fused_computation.29 | convolution fusion | flops 6444810240 | bytes 7340032 | tf_op jit(solution)/shard_map/dot_general | solution.py:75
  374.0 2.5 broadcast_in_dim.16
  376.5 0.0 copy-done.4
  376.5 5.2 %scatter_fusion = bf16[32,32,4,512]{3,1,2,0:T(8,128)(2,1)} fusion(bf16[32,32,4,512]{3,1,2,0:T(8,128)(2,1)} %broadcast_in_dim.16, s32[16]{0:T(128)S(1)} %fusion.48, bf16[16,32,4,512]{3,1,2,0:T(8,128)(2,1)S(1)} %copy-done.4), kind=kCustom, calls=%fused_computation.2 | custom fusion | bytes 6291520 | tf_op jit(solution)/shard_map/scatter | solution.py:77
  381.7 9.4 %all-to-all-start.1 = ((bf16[32,32,4,512]{3,1,2,0:T(8,128)(2,1)}), bf16[32,32,4,512]{3,1,2,0:T(8,128)(2,1)}, u32[]{:S(2)}, u32[]{:S(2)}) async-start(bf16[32,32,4,512]{3,1,2,0:T(8,128)(2,1)} %scatter_fusion), calls=%async_computation.2 | async-start | bytes 8388608 | tf_op jit(solution)/shard_map/all_to_all | solution.py:78
  391.1 0.9 copy.86
  391.9 93.8 %all-to-all-done.1 = bf16[32,32,4,512]{3,1,2,0:T(8,128)(2,1)} async-done(((bf16[32,32,4,512]{3,1,2,0:T(8,128)(2,1)}), bf16[32,32,4,512]{3,1,2,0:T(8,128)(2,1)}, u32[]{:S(2)}, u32[]{:S(2)}) %all-to-all-start.1) | async-done | bytes 4194336 | tf_op jit(solution)/shard_map/all_to_all | solution.py:78
  485.7 8.1 %copy.81 = bf16[32,32,4,512]{3,2,1,0:T(4,128)(2,1)} copy(bf16[32,32,4,512]{3,1,2,0:T(8,128)(2,1)} %all-to-all-done.1) | data formatting | bytes 8388608 | tf_op jit(solution)/shard_map/all_to_all | solution.py:78
  493.8 6.3 %reshape.108 = bf16[32,65536]{1,0:T(8,128)(2,1)} reshape(bf16[32,32,4,512]{3,2,1,0:T(4,128)(2,1)} %copy.81) | data formatting | bytes 8388608 | tf_op jit(solution)/shard_map/reshape | solution.py:79
  500.1 6.7 %dot_general.48 = bf16[32,4,512,32]{2,1,0,3:T(4,128)(2,1)} reshape(bf16[65536,32]{0,1:T(8,128)(2,1)} %bitcast.118) | data formatting | bytes 8388608 | tf_op jit(solution)/shard_map/dot_general | solution.py:80
  506.8 0.0 copy-done.6
  506.8 4.9 fusion.57
  511.7 0.9 copy.84
  512.7 0.8 copy.85
  (12 shorter events, 0.0 us)
Async XLA Ops:
  17.0 11.3 %copy-start.5 = (bf16[1,16,2,4,32,256]{5,4,3,2,1,0:T(8,128)(2,1)S(1)}, bf16[1,16,2,4,32,256]{5,4,3,2,1,0:T(8,128)(2,1)}, u32[]{:S(2)}) copy-start(bf16[1,16,2,4,32,256]{5,4,3,2,1,0:T(8,128)(2,1)} %param.5) | copy-start | bytes 6291460
  17.0 105.9 %all-to-all-start = ((bf16[32,32,4,512]{3,1,2,0:T(8,128)(2,1)}), bf16[32,32,4,512]{3,1,2,0:T(8,128)(2,1)}, u32[]{:S(2)}, u32[]{:S(2)}) async-start(bf16[32,32,4,512]{3,1,2,0:T(8,128)(2,1)} %broadcast_select_fusion), calls=%async_computation | async-start | bytes 8388608 | tf_op jit(solution)/shard_map/all_to_all | solution.py:47
  28.3 224.9 %reduce-scatter.2.cloned.1.call-start = ((), (), s32[]{:S(2)}) async-start(), calls=%async_computation.3 | async-start | bytes 2359296 | tf_op jit(solution)/shard_map/reduce_scatter | solution.py:63
  28.3 12.0 %copy-start.8 = (s32[32,16]{0,1:T(8,128)S(1)}, s32[32,16]{0,1:T(8,128)}, u32[]{:S(2)}) copy-start(s32[32,16]{0,1:T(8,128)} %param.7) | copy-start | bytes 6148
  140.4 6.9 %copy-start.1 = (bf16[16,32,4,256]{1,0,2,3:T(8,128)(2,1)S(1)}, bf16[16,32,4,256]{1,0,2,3:T(8,128)(2,1)}, u32[]{:S(2)}) copy-start(bf16[16,32,4,256]{1,0,2,3:T(8,128)(2,1)} %copy.73) | copy-start | bytes 3145732
  140.5 10.6 %slice-start = ((s8[8388608]{0:T(1024)(128)(4,1)}), s8[4194304]{0:T(1024)(128)(4,1)S(1)}, s32[]{:S(2)}) async-start(s8[8388608]{0:T(1024)(128)(4,1)} %bitcast.114), calls=%async_computation.5 | async-start | bytes 8388608
  147.3 3.7 slice-start.1
  151.1 5.7 %copy-start = (bf16[16,32,4,256]{1,0,2,3:T(8,128)(2,1)S(1)}, bf16[16,32,4,256]{1,0,2,3:T(8,128)(2,1)}, u32[]{:S(2)}) copy-start(bf16[16,32,4,256]{1,0,2,3:T(8,128)(2,1)} %copy.72) | copy-start | bytes 3145732
  156.8 3.2 copy-start.2
  166.5 86.7 %copy-start.7 = (bf16[1,2,32,4,256]{4,3,2,1,0:T(4,128)(2,1)S(1)}, bf16[1,2,32,4,256]{4,3,2,1,0:T(4,128)(2,1)}, u32[]{:S(2)}) copy-start(bf16[1,2,32,4,256]{4,3,2,1,0:T(4,128)(2,1)} %param.6) | copy-start | bytes 393220
  174.5 132.2 %all-gather.2.cloned.1.call-start = ((), (), s32[]{:S(2)}) async-start(), calls=%async_computation.4 | async-start | bytes 1179648 | tf_op jit(solution)/shard_map/all_gather | solution.py:65
  356.9 7.6 %copy-start.3 = (f32[16,32,4,256]{3,1,2,0:T(8,128)S(1)}, f32[16,32,4,256]{3,1,2,0:T(8,128)}, u32[]{:S(2)}) copy-start(f32[16,32,4,256]{3,1,2,0:T(8,128)} %copy.79) | copy-start | bytes 6291460
  374.0 2.5 copy-start.4
  381.7 104.0 %all-to-all-start.1 = ((bf16[32,32,4,512]{3,1,2,0:T(8,128)(2,1)}), bf16[32,32,4,512]{3,1,2,0:T(8,128)(2,1)}, u32[]{:S(2)}, u32[]{:S(2)}) async-start(bf16[32,32,4,512]{3,1,2,0:T(8,128)(2,1)} %scatter_fusion), calls=%async_computation.2 | async-start | bytes 8388608 | tf_op jit(solution)/shard_map/all_to_all | solution.py:78
  500.1 6.7 %copy-start.6 = (f32[2,32,4,512]{3,2,1,0:T(4,128)S(1)}, f32[2,32,4,512]{3,2,1,0:T(4,128)}, u32[]{:S(2)}) copy-start(f32[2,32,4,512]{3,2,1,0:T(4,128)} %param.4) | copy-start | bytes 1572868
Sparse Core Ops, SparseCore 0:
  174.6 78.5 reduce-scatter.1
  256.4 50.2 all-gather.1

commit v2 on v0

v2 whole, which is shorter than its diff:
```python
import math

import jax
import jax.numpy as jnp
from jax import lax
from jax.sharding import PartitionSpec as P

step_length = 0.5
chunks = 2


def make_table(samples):
    freqs = samples // 2
    sample_index = lax.broadcasted_iota(jnp.int32, (samples, freqs), 0)
    freq_index = lax.broadcasted_iota(jnp.int32, (samples, freqs), 1)
    phase = (sample_index * freq_index % samples).astype(jnp.float32) * (2.0 * math.pi / samples)
    return jnp.concatenate([jnp.cos(phase), -jnp.sin(phase)], axis=1)


def contract(spec, listed):
    return jnp.einsum("lakf,lkrf->arf", spec, listed, preferred_element_type=jnp.float32)


def correlate(misfit_part, listed):
    return jnp.einsum("arf,lkrf->lakf", misfit_part, listed, preferred_element_type=jnp.float32)


def per_device(response, data_spectra, observed, block_lists):
    owners = lax.axis_size("target")
    channels = lax.axis_size("surface")
    my_index = lax.axis_index("target")
    owned = response.shape[0]
    shots = response.shape[1]
    samples = response.shape[3]
    freqs = samples // 2
    dft_table = make_table(samples)
    table_half = dft_table.astype(jnp.bfloat16)
    own_ids = lax.dynamic_slice_in_dim(block_lists, my_index, 1, 0)[0]
    own_owner = own_ids // owned
    wanted = block_lists // owned == my_index
    present = jnp.any(wanted, axis=1)
    slot_for = jnp.sum(jnp.where(wanted, block_lists % owned, 0), axis=1)
    picker = (
        (slot_for[None, :] == jnp.arange(owned, dtype=jnp.int32)[:, None]) & present[None, :]
    ).astype(jnp.bfloat16)
    present_rows = present[:, None, None, None]
    zero_half = jnp.zeros((), jnp.bfloat16)
    copy_now = response.astype(jnp.bfloat16)
    listed_data = data_spectra[0]
    data_real = listed_data[:, 0]
    data_imag = listed_data[:, 1]
    observed_all = observed[0].astype(jnp.float32)
    width = shots // chunks
    next_parts, copy_parts, residual_parts = [], [], []
    for c in range(chunks):
        lo, hi = c * width, (c + 1) * width
        outgoing = jnp.where(present_rows, copy_now[slot_for, lo:hi], zero_half)
        arrived = lax.all_to_all(outgoing, "target", split_axis=0, concat_axis=0, tiled=True)
        spectra = jnp.dot(arrived[own_owner], table_half, preferred_element_type=jnp.float32).astype(
            jnp.bfloat16
        )
        spec_real = spectra[..., :freqs]
        spec_imag = spectra[..., freqs:]
        partial_value = jnp.stack(
            [
                contract(spec_real, data_real) - contract(spec_imag, data_imag),
                contract(spec_real, data_imag) + contract(spec_imag, data_real),
            ]
        )
        recvs = partial_value.shape[2]
        split_value = partial_value.reshape(2, width, channels, recvs // channels, freqs)
        exchanged = lax.all_to_all(split_value, "surface", split_axis=2, concat_axis=2, tiled=True)
        summed_share = jnp.sum(exchanged, axis=2)
        residual_share = observed_all[:, lo:hi] - summed_share
        misfit_share = residual_share.astype(jnp.bfloat16)
        spread = jnp.broadcast_to(misfit_share[None], (channels,) + misfit_share.shape)
        gathered = lax.all_to_all(spread, "surface", split_axis=0, concat_axis=0, tiled=True)
        misfit = jnp.moveaxis(gathered, 0, 2).reshape(2, width, recvs, freqs)
        misfit_real = misfit[0]
        misfit_imag = misfit[1]
        grad_spectra = jnp.concatenate(
            [
                -(correlate(misfit_real, data_real) + correlate(misfit_imag, data_imag)),
                correlate(misfit_real, data_imag) - correlate(misfit_imag, data_real),
            ],
            axis=-1,
        )
        grad_time = jnp.dot(grad_spectra, dft_table.T, precision=lax.Precision.HIGHEST)
        grad_half = grad_time.astype(jnp.bfloat16)
        returning = jnp.zeros((owners,) + grad_time.shape[1:], jnp.bfloat16).at[own_owner].set(grad_half)
        received = lax.all_to_all(returning, "target", split_axis=0, concat_axis=0, tiled=True)
        flat = received.reshape(owners, -1)
        gradient = jnp.dot(picker, flat, preferred_element_type=jnp.float32).reshape(
            (owned, width) + response.shape[2:]
        )
        response_next = response[:, lo:hi] - step_length * gradient
        next_parts.append(response_next)
        copy_parts.append(response_next.astype(jnp.bfloat16))
        residual_parts.append(residual_share)
    response_next = jnp.concatenate(next_parts, axis=1)
    response_copy = jnp.concatenate(copy_parts, axis=1)
    residual = jnp.concatenate(residual_parts, axis=1)
    return (response_next, response_copy, residual[None])


def solution(mesh):
    return jax.shard_map(
        per_device,
        mesh=mesh,
        in_specs=(
            P("target", None, "surface", None),
            P("target", None, None, "surface", None, None),
            P("target", None, None, "surface", None),
            P(),
        ),
        out_specs=(
            P("target", None, "surface", None),
            P("target", None, "surface", None),
            P("target", None, None, "surface", None),
        ),
        check_vma=False,
    )
```

time: 656 us -> 511 us (0.78)
  waiting for transfers between devices: 394 us -> 47.2 us
  matrix products: 72.7 us -> 185 us
  blocking collectives: 0 us -> 75.7 us
  starting transfers between devices: 21.3 us -> 43.7 us
  between operations: 14.7 us -> 1.47 us
  local copies, waits for them, and re-layouts: 129 us -> 137 us
    all_to_all x1 -> x2, waiting for transfers between devices: 183 us -> 34.5 us  [per_device(): lax.all_to_all(returning, 'target', split_axis=0, concat_axis=0, tiled=True)]
    dot_general x4 -> x8, matrix products: 31.6 us -> 119 us  [correlate(): jnp.einsum('arf,lkrf->lakf', misfit_part, listed, preferred_element_type=...]
    all_to_all x1, waiting for transfers between devices: 80.1 us -> 0.01 us  [per_device(): lax.all_to_all(outgoing, 'target', split_axis=0, concat_axis=0, tiled=True)]
    reduce_scatter x1 -> x0, waiting for transfers between devices: 78.7 us -> none  [per_device(): lax.psum_scatter(partial_value, 'surface', scatter_dimension=2, tiled=True)]
    all_to_all x0 -> x2, blocking collectives: none -> 75.7 us  [the longest x1 59.8 us: per_device(): lax.all_to_all(outgoing, 'target', split_axis=0, concat_axis=0, tiled=True)]
    all_gather x1 -> x0, waiting for transfers between devices: 51.8 us -> none  [per_device(): lax.all_gather(residual_share.astype(jnp.bfloat16), 'surface', axis=2, ti...]
    dot_general x4 -> x8, matrix products: 19.5 us -> 48.2 us  [contract(): jnp.einsum('lakf,lkrf->arf', spec, listed, preferred_element_type=jnp.flo...]
    all_to_all x0 -> x3, starting transfers between devices: none -> 17.9 us  [the longest x2 13.5 us: per_device(): lax.all_to_all(split_value, 'surface', split_axis=2, concat_axis=2, tiled...]
  transfers between devices with their start and end apart: 4 -> 6, of which waited for: 4 -> 2; matrix products, arithmetic and copies ran while one was open for 2% -> 60% of each run, Pallas kernels for 0% -> 0%
where the time goes in v2:
time: 511 us; the launch traced here: 503 us
  matrix products  185 us (36%)
  local copies, waits for them, and re-layouts  137 us (27%)
  blocking collectives  75.7 us (15%)
  waiting for transfers between devices  47.2 us (9%)
  starting transfers between devices  43.7 us (9%)
  other arithmetic  12.8 us (3%)
    dot_general x8, matrix products, correlate(): jnp.einsum('arf,lkrf->lakf', misfit_part, listed, preferred_element_type=...  119 us
    all_to_all x1, blocking collectives, per_device(): lax.all_to_all(outgoing, 'target', split_axis=0, concat_axis=0, tiled=True)  59.8 us
    dot_general x8, matrix products, contract(): jnp.einsum('lakf,lkrf->arf', spec, listed, preferred_element_type=jnp.flo...  48.2 us
    all_to_all x2, waiting for transfers between devices, per_device(): lax.all_to_all(returning, 'target', split_axis=0, concat_axis=0, tiled=True)  34.5 us
    all_to_all x2, starting transfers between devices, per_device(): lax.all_to_all(returning, 'target', split_axis=0, concat_axis=0, tiled=True)  18.9 us
    slice x4, local copies, waits for them, and re-layouts, per_device(): spec_imag = spectra[..., freqs:]  16.4 us
    unnamed x23, local copies, waits for them, and re-layouts  16.4 us
    all_to_all x1, blocking collectives, per_device(): lax.all_to_all(spread, 'surface', split_axis=0, concat_axis=0, tiled=True)  15.9 us
  transfers between devices with their start and end apart: 6, of which 2 were waited for; matrix products, arithmetic and copies ran while one was open for 60% of the time, Pallas kernels for 0%

profile of v2, /device:TPU:1, one launch (start us, length us, event | category | flops | bytes accessed | tf_op | source)
XLA Modules:
  0.0 502.8 jit_solution(17661699371980346386)
XLA Ops:
  2.1 1.1 copy.204
  3.2 2.4 gather_fusion
  5.6 3.6 gather_fusion.2
  9.1 4.1 broadcast_select_fusion.1
  13.3 59.8 %all_to_all.40 = bf16[32,16,4,512]{3,2,1,0:T(4,128)(2,1)S(1)} all-to-all(bf16[32,16,4,512]{3,2,1,0:T(4,128)(2,1)S(1)} %get-tuple-element.34), channel_id=1, replica_groups=mesh['target'=32,'surface'=8] {'target'}, dimensions={0} | all-to-all | bytes 4194304 | tf_op jit(solution)/shard_map/all_to_all | solution.py:58
  73.0 6.9 %all-to-all-start = ((bf16[32,16,4,512]{3,2,1,0:T(4,128)(2,1)}), bf16[32,16,4,512]{3,2,1,0:T(4,128)(2,1)}, u32[]{:S(2)}, u32[]{:S(2)}) async-start(bf16[32,16,4,512]{3,2,1,0:T(4,128)(2,1)} %get-tuple-element.33), calls=%async_computation | async-start | bytes 4194304 | tf_op jit(solution)/shard_map/all_to_all | solution.py:58
  79.9 12.6 %copy.101 = bf16[1,16,2,4,32,256]{4,1,3,5,2,0:T(8,128)(2,1)} copy(bf16[1,16,2,4,32,256]{5,4,3,2,1,0:T(8,128)(2,1)} %param.5) | data formatting | bytes 4194304 | tf_op args[1]
  92.8 2.1 sine_negate_fusion
  94.9 2.4 gather_fusion.3
  97.3 1.9 convolution_convert_fusion
  99.4 6.6 %copy.122 = bf16[16,16,4,256]{0,1,2,3:T(8,128)(2,1)} copy(bf16[16,16,4,256]{3,1,2,0:T(8,128)(2,1)S(1)} %get-tuple-element.24) | data formatting | bytes 1048576 | tf_op jit(solution)/shard_map/slice | solution.py:62
  106.0 6.8 %copy.123 = bf16[16,16,4,256]{0,1,2,3:T(8,128)(2,1)} copy(bf16[16,16,4,256]{3,1,2,0:T(8,128)(2,1)S(1)} %get-tuple-element.23) | data formatting | bytes 1048576 | tf_op jit(solution)/shard_map/slice | solution.py:63
  112.8 6.2 %fusion.39 = f32[256,16,32,1]{2,1,3,0:T(8,128)S(1)} fusion(bf16[16,16,4,256]{0,1,2,3:T(8,128)(2,1)} %copy.122, bf16[16,2,4,32,256]{3,0,2,4,1:T(8,128)(2,1)} %bitcast.168), kind=kOutput, calls=%fused_computation.53 | convolution fusion | flops 16777216 | bytes 8912896 | tf_op jit(solution)/shard_map/lakf,lkrf->arf/dot_general | solution.py:21
  119.0 5.0 fusion.9
  124.0 2.0 copy.124
  126.0 6.2 %fusion.43 = f32[256,16,32,1]{2,1,3,0:T(8,128)S(1)} fusion(bf16[16,16,4,256]{0,1,2,3:T(8,128)(2,1)} %copy.122, bf16[16,2,4,32,256]{3,0,2,4,1:T(8,128)(2,1)} %bitcast.170), kind=kOutput, calls=%fused_computation.57 | convolution fusion | flops 16777216 | bytes 8912896 | tf_op jit(solution)/shard_map/lakf,lkrf->arf/dot_general | solution.py:21
  132.2 5.0 fusion.8
  137.1 2.0 copy.127
  139.1 1.3 pad_maximum_fusion.2
  141.5 6.9 %all-to-all-start.5 = ((f32[2,16,8,4,256]{4,1,3,0,2:T(8,128)}), f32[2,16,8,4,256]{4,1,3,0,2:T(8,128)}, u32[]{:S(2)}, u32[]{:S(2)}) async-start(f32[2,16,8,4,256]{4,1,3,0,2:T(8,128)} %copy.128), calls=%async_computation.5 | async-start | bytes 2097152 | tf_op jit(solution)/shard_map/all_to_all | solution.py:72
  148.4 3.0 gather_fusion.1
  153.0 6.6 %copy.102 = bf16[16,16,4,256]{0,1,2,3:T(8,128)(2,1)} copy(bf16[16,16,4,256]{3,1,2,0:T(8,128)(2,1)S(1)} %get-tuple-element.22) | data formatting | bytes 1048576 | tf_op jit(solution)/shard_map/slice | solution.py:62
  159.6 6.1 %fusion.41 = f32[256,16,32,1]{2,1,3,0:T(8,128)S(1)} fusion(bf16[16,16,4,256]{0,1,2,3:T(8,128)(2,1)} %copy.102, bf16[16,2,4,32,256]{3,0,2,4,1:T(8,128)(2,1)} %bitcast.172), kind=kOutput, calls=%fused_computation.55 | convolution fusion | flops 16777216 | bytes 8912896 | tf_op jit(solution)/shard_map/lakf,lkrf->arf/dot_general | solution.py:21
  165.7 8.6 %copy.103 = bf16[16,16,4,256]{0,1,2,3:T(8,128)(2,1)} copy(bf16[16,16,4,256]{3,1,2,0:T(8,128)(2,1)} %get-tuple-element.21) | data formatting | bytes 1048576 | tf_op jit(solution)/shard_map/slice | solution.py:63
  174.3 7.6 %fusion.11 = f32[16,32,256]{1,0,2:T(8,128)} fusion(f32[256,16,32,1]{2,1,3,0:T(8,128)S(1)} %fusion.41, bf16[16,16,4,256]{0,1,2,3:T(8,128)(2,1)} %copy.103, bf16[16,2,4,32,256]{3,0,2,4,1:T(8,128)(2,1)} %bitcast.173), kind=kOutput, calls=%fused_computation.27 | convolution fusion | flops 16908288 | bytes 9437184 | tf_op jit(solution)/shard_map/lakf,lkrf->arf/dot_general | solution.py:21
  181.9 4.8 fusion.45
  186.7 3.5 copy.104
  190.2 7.4 %fusion.10 = f32[16,32,256]{1,0,2:T(8,128)} fusion(f32[256,16,32,1]{2,1,3,0:T(8,128)S(1)} %fusion.45, bf16[16,16,4,256]{0,1,2,3:T(8,128)(2,1)} %copy.103, bf16[16,2,4,32,256]{3,0,2,4,1:T(8,128)(2,1)} %bitcast.175), kind=kOutput, calls=%fused_computation.25 | convolution fusion | flops 16908288 | bytes 9437184 | tf_op jit(solution)/shard_map/lakf,lkrf->arf/dot_general | solution.py:21
  197.6 2.7 copy.107
  200.3 1.1 pad_maximum_fusion.1
  202.5 6.7 %all-to-all-start.1 = ((f32[2,16,8,4,256]{4,1,3,0,2:T(8,128)}), f32[2,16,8,4,256]{4,1,3,0,2:T(8,128)S(1)}, u32[]{:S(2)}, u32[]{:S(2)}) async-start(f32[2,16,8,4,256]{4,1,3,0,2:T(8,128)} %copy.108), calls=%async_computation.1 | async-start | bytes 2097152 | tf_op jit(solution)/shard_map/all_to_all | solution.py:72
  209.2 1.3 reduce_sum.32
  210.5 12.7 %all-to-all-done.1 = f32[2,16,8,4,256]{4,1,3,0,2:T(8,128)S(1)} async-done(((f32[2,16,8,4,256]{4,1,3,0,2:T(8,128)}), f32[2,16,8,4,256]{4,1,3,0,2:T(8,128)S(1)}, u32[]{:S(2)}, u32[]{:S(2)}) %all-to-all-start.1) | async-done | bytes 1048608 | tf_op jit(solution)/shard_map/all_to_all | solution.py:72
  224.0 15.9 %all_to_all.41 = bf16[8,2,16,4,256]{4,2,3,1,0:T(8,128)(2,1)S(1)} all-to-all(bf16[8,2,16,4,256]{4,2,3,1,0:T(8,128)(2,1)S(1)} %broadcast_in_dim.23), channel_id=1, replica_groups=mesh['target'=32,'surface'=8] {'surface'}, dimensions={0} | all-to-all | bytes 1048576 | tf_op jit(solution)/shard_map/all_to_all | solution.py:77
  240.8 4.4 all-to-all-start.6
  246.3 15.3 %fusion.40 = f32[256,16,16,4]{2,1,3,0:T(8,128)} fusion(bf16[16,32,256,1]{1,0,3,2:T(8,128)(2,1)S(1)} %copy.148, bf16[16,2,4,32,256]{3,0,2,4,1:T(8,128)(2,1)} %bitcast.176), kind=kOutput, calls=%fused_computation.54 | convolution fusion | flops 16777216 | bytes 5505024 | tf_op jit(solution)/shard_map/arf,lkrf->lakf/dot_general | solution.py:25
  261.6 15.3 %fusion.44 = f32[256,16,16,4]{2,1,3,0:T(8,128)} fusion(bf16[16,32,256,1]{1,0,3,2:T(8,128)(2,1)S(1)} %copy.148, bf16[16,2,4,32,256]{3,0,2,4,1:T(8,128)(2,1)} %bitcast.177), kind=kOutput, calls=%fused_computation.58 | convolution fusion | flops 16777216 | bytes 5505024 | tf_op jit(solution)/shard_map/arf,lkrf->lakf/dot_general | solution.py:25
  277.9 18.3 %negate_bitcast_fusion.1 = f32[16,16,4,256]{0,1,2,3:T(8,128)} fusion(f32[256,16,16,4]{2,1,3,0:T(8,128)} %fusion.40, bf16[16,32,256,1]{1,0,3,2:T(8,128)(2,1)S(1)} %copy.149, bf16[16,2,4,32,256]{3,0,2,4,1:T(8,128)(2,1)} %bitcast.178), kind=kOutput, calls=%fused_computation.9 | convolution fusion | flops 17301504 | bytes 13893632 | tf_op jit(solution)/shard_map/arf,lkrf->lakf/dot_general | solution.py:25
  296.2 15.4 %subtract_bitcast_fusion.1 = f32[16,16,4,256]{0,1,2,3:T(8,128)} fusion(f32[256,16,16,4]{2,1,3,0:T(8,128)S(1)} %copy-done.3, bf16[16,32,256,1]{1,0,3,2:T(8,128)(2,1)S(1)} %copy.149, bf16[16,2,4,32,256]{3,0,2,4,1:T(8,128)(2,1)} %bitcast.179), kind=kOutput, calls=%fused_computation.8 | convolution fusion | flops 17039360 | bytes 6553600 | tf_op jit(solution)/shard_map/arf,lkrf->lakf/dot_general | solution.py:25
  311.7 6.6 %copy.115 = f32[16,16,4,256]{3,1,2,0:T(8,128)S(1)} copy(f32[16,16,4,256]{0,1,2,3:T(8,128)} %negate_bitcast_fusion.1) | data formatting | bytes 2097152 | tf_op jit(solution)/shard_map/neg | solution.py:83
  318.3 6.6 %copy.116 = f32[16,16,4,256]{3,1,2,0:T(8,128)S(1)} copy(f32[16,16,4,256]{0,1,2,3:T(8,128)} %subtract_bitcast_fusion.1) | data formatting | bytes 2097152 | tf_op jit(solution)/shard_map/sub | solution.py:84
  324.9 4.5 fusion.19
  329.5 1.6 broadcast.125.clone2.1
  331.1 3.4 scatter_fusion
  334.5 10.3 %all-to-all-start.3 = ((bf16[32,16,4,512]{3,1,2,0:T(8,128)(2,1)}), bf16[32,16,4,512]{3,1,2,0:T(8,128)(2,1)}, u32[]{:S(2)}, u32[]{:S(2)}) async-start(bf16[32,16,4,512]{3,1,2,0:T(8,128)(2,1)} %scatter_fusion), calls=%async_computation.3 | async-start | bytes 4194304 | tf_op jit(solution)/shard_map/all_to_all | solution.py:91
  348.0 12.0 %fusion.38 = f32[256,16,16,4]{2,1,3,0:T(8,128)S(1)} fusion(bf16[16,32,256,1]{1,0,3,2:T(8,128)(2,1)S(1)} %copy.158, bf16[16,2,4,32,256]{3,0,2,4,1:T(8,128)(2,1)} %bitcast.180), kind=kOutput, calls=%fused_computation.52 | convolution fusion | flops 16777216 | bytes 5505024 | tf_op jit(solution)/shard_map/arf,lkrf->lakf/dot_general | solution.py:25
  360.0 15.4 %negate_bitcast_fusion = f32[16,16,4,256]{0,1,2,3:T(8,128)} fusion(f32[256,16,16,4]{2,1,3,0:T(8,128)S(1)} %fusion.38, bf16[16,32,256,1]{1,0,3,2:T(8,128)(2,1)S(1)} %copy.159, bf16[16,2,4,32,256]{3,0,2,4,1:T(8,128)(2,1)} %bitcast.181), kind=kOutput, calls=%fused_computation.7 | convolution fusion | flops 17301504 | bytes 6553600 | tf_op jit(solution)/shard_map/arf,lkrf->lakf/dot_general | solution.py:25
  375.5 7.6 %copy.135 = f32[16,16,4,256]{3,1,2,0:T(8,128)} copy(f32[16,16,4,256]{0,1,2,3:T(8,128)} %negate_bitcast_fusion) | data formatting | bytes 2097152 | tf_op jit(solution)/shard_map/neg | solution.py:83
  383.1 12.0 %fusion.42 = f32[256,16,16,4]{2,1,3,0:T(8,128)S(1)} fusion(bf16[16,32,256,1]{1,0,3,2:T(8,128)(2,1)S(1)} %copy.158, bf16[16,2,4,32,256]{3,0,2,4,1:T(8,128)(2,1)} %bitcast.182), kind=kOutput, calls=%fused_computation.56 | convolution fusion | flops 16777216 | bytes 5505024 | tf_op jit(solution)/shard_map/arf,lkrf->lakf/dot_general | solution.py:25
  395.1 15.5 %subtract_bitcast_fusion = f32[16,16,4,256]{0,1,2,3:T(8,128)} fusion(f32[256,16,16,4]{2,1,3,0:T(8,128)S(1)} %fusion.42, bf16[16,32,256,1]{1,0,3,2:T(8,128)(2,1)S(1)} %copy.159, bf16[16,2,4,32,256]{3,0,2,4,1:T(8,128)(2,1)} %bitcast.183), kind=kOutput, calls=%fused_computation.6 | convolution fusion | flops 17039360 | bytes 6553600 | tf_op jit(solution)/shard_map/arf,lkrf->lakf/dot_general | solution.py:25
  410.6 6.7 %copy.136 = f32[16,16,4,256]{3,1,2,0:T(8,128)S(1)} copy(f32[16,16,4,256]{0,1,2,3:T(8,128)} %subtract_bitcast_fusion) | data formatting | bytes 2097152 | tf_op jit(solution)/shard_map/sub | solution.py:84
  417.3 4.5 fusion.16
  421.8 1.6 broadcast.125.clone2
  423.4 3.4 scatter_fusion.1
  426.8 8.6 %all-to-all-start.7 = ((bf16[32,16,4,512]{3,1,2,0:T(8,128)(2,1)}), bf16[32,16,4,512]{3,1,2,0:T(8,128)(2,1)S(1)}, u32[]{:S(2)}, u32[]{:S(2)}) async-start(bf16[32,16,4,512]{3,1,2,0:T(8,128)(2,1)} %scatter_fusion.1), calls=%async_computation.7 | async-start | bytes 4194304 | tf_op jit(solution)/shard_map/all_to_all | solution.py:91
  436.4 4.9 copy.118
  441.3 4.5 reshape.135
  445.8 4.5 dot_general.85
  450.3 34.5 %all-to-all-done.7 = bf16[32,16,4,512]{3,1,2,0:T(8,128)(2,1)S(1)} async-done(((bf16[32,16,4,512]{3,1,2,0:T(8,128)(2,1)}), bf16[32,16,4,512]{3,1,2,0:T(8,128)(2,1)S(1)}, u32[]{:S(2)}, u32[]{:S(2)}) %all-to-all-start.7) | async-done | bytes 2097184 | tf_op jit(solution)/shard_map/all_to_all | solution.py:91
  484.8 3.3 copy.138
  488.1 3.3 reshape.136
  491.3 2.8 dot_general.98
  494.1 3.0 fusion.86
  497.1 3.0 fusion.85
  (53 shorter events, 15.9 us)
Async XLA Ops:
  73.0 68.5 %all-to-all-start = ((bf16[32,16,4,512]{3,2,1,0:T(4,128)(2,1)}), bf16[32,16,4,512]{3,2,1,0:T(4,128)(2,1)}, u32[]{:S(2)}, u32[]{:S(2)}) async-start(bf16[32,16,4,512]{3,2,1,0:T(4,128)(2,1)} %get-tuple-element.33), calls=%async_computation | async-start | bytes 4194304 | tf_op jit(solution)/shard_map/all_to_all | solution.py:58
  79.9 12.7 %copy-start.8 = (s32[32,16]{0,1:T(8,128)S(1)}, s32[32,16]{0,1:T(8,128)}, u32[]{:S(2)}) copy-start(s32[32,16]{0,1:T(8,128)} %param.7) | copy-start | bytes 6148
  112.8 6.2 %copy-start = (bf16[16,16,4,256]{0,1,2,3:T(8,128)(2,1)S(1)}, bf16[16,16,4,256]{0,1,2,3:T(8,128)(2,1)}, u32[]{:S(2)}) copy-start(bf16[16,16,4,256]{0,1,2,3:T(8,128)(2,1)} %copy.123) | copy-start | bytes 1572868
  126.0 6.2 %copy-start.1 = (bf16[16,16,4,256]{0,1,2,3:T(8,128)(2,1)S(1)}, bf16[16,16,4,256]{0,1,2,3:T(8,128)(2,1)}, u32[]{:S(2)}) copy-start(bf16[16,16,4,256]{0,1,2,3:T(8,128)(2,1)} %copy.123) | copy-start | bytes 1572868
  141.5 61.0 %all-to-all-start.5 = ((f32[2,16,8,4,256]{4,1,3,0,2:T(8,128)}), f32[2,16,8,4,256]{4,1,3,0,2:T(8,128)}, u32[]{:S(2)}, u32[]{:S(2)}) async-start(f32[2,16,8,4,256]{4,1,3,0,2:T(8,128)} %copy.128), calls=%async_computation.5 | async-start | bytes 2097152 | tf_op jit(solution)/shard_map/all_to_all | solution.py:72
  174.3 7.6 %copy-start.2 = (bf16[16,16,4,256]{0,1,2,3:T(8,128)(2,1)S(1)}, bf16[16,16,4,256]{0,1,2,3:T(8,128)(2,1)}, u32[]{:S(2)}) copy-start(bf16[16,16,4,256]{0,1,2,3:T(8,128)(2,1)} %copy.102) | copy-start | bytes 1572868
  197.6 11.6 %copy-start.7 = (bf16[1,2,32,4,256]{4,3,2,1,0:T(4,128)(2,1)S(1)}, bf16[1,2,32,4,256]{4,3,2,1,0:T(4,128)(2,1)}, u32[]{:S(2)}) copy-start(bf16[1,2,32,4,256]{4,3,2,1,0:T(4,128)(2,1)} %param.6) | copy-start | bytes 393220
  202.5 20.7 %all-to-all-start.1 = ((f32[2,16,8,4,256]{4,1,3,0,2:T(8,128)}), f32[2,16,8,4,256]{4,1,3,0,2:T(8,128)S(1)}, u32[]{:S(2)}, u32[]{:S(2)}) async-start(f32[2,16,8,4,256]{4,1,3,0,2:T(8,128)} %copy.108), calls=%async_computation.1 | async-start | bytes 2097152 | tf_op jit(solution)/shard_map/all_to_all | solution.py:72
  240.8 93.7 %all-to-all-start.6 = ((bf16[8,2,16,4,256]{4,2,3,1,0:T(8,128)(2,1)}), bf16[8,2,16,4,256]{4,2,3,1,0:T(8,128)(2,1)}, u32[]{:S(2)}, u32[]{:S(2)}) async-start(bf16[8,2,16,4,256]{4,2,3,1,0:T(8,128)(2,1)} %broadcast_in_dim.24), calls=%async_computation.6 | async-start | bytes 1048576 | tf_op jit(solution)/shard_map/all_to_all | solution.py:77
  277.9 18.3 %copy-start.3 = (f32[256,16,16,4]{2,1,3,0:T(8,128)S(1)}, f32[256,16,16,4]{2,1,3,0:T(8,128)}, u32[]{:S(2)}) copy-start(f32[256,16,16,4]{2,1,3,0:T(8,128)} %fusion.44) | copy-start | bytes 3145732
  334.5 92.3 %all-to-all-start.3 = ((bf16[32,16,4,512]{3,1,2,0:T(8,128)(2,1)}), bf16[32,16,4,512]{3,1,2,0:T(8,128)(2,1)}, u32[]{:S(2)}, u32[]{:S(2)}) async-start(bf16[32,16,4,512]{3,1,2,0:T(8,128)(2,1)} %scatter_fusion), calls=%async_computation.3 | async-start | bytes 4194304 | tf_op jit(solution)/shard_map/all_to_all | solution.py:91
  410.6 6.7 %copy-start.4 = (f32[16,16,4,256]{3,1,2,0:T(8,128)S(1)}, f32[16,16,4,256]{3,1,2,0:T(8,128)}, u32[]{:S(2)}) copy-start(f32[16,16,4,256]{3,1,2,0:T(8,128)} %copy.135) | copy-start | bytes 3145732
  423.4 12.1 %copy-start.5 = (f32[2,32,4,512]{3,2,1,0:T(4,128)S(1)}, f32[2,32,4,512]{3,2,1,0:T(4,128)}, u32[]{:S(2)}) copy-start(f32[2,32,4,512]{3,2,1,0:T(4,128)} %param.4) | copy-start | bytes 1572868
  423.4 12.1 %copy-start.6 = (f32[2,16,4,256]{3,1,2,0:T(8,128)S(1)}, f32[2,16,4,256]{3,1,2,0:T(8,128)}, u32[]{:S(2)}) copy-start(f32[2,16,4,256]{3,1,2,0:T(8,128)} %get-tuple-element.32) | copy-start | bytes 393220
  426.8 58.0 %all-to-all-start.7 = ((bf16[32,16,4,512]{3,1,2,0:T(8,128)(2,1)}), bf16[32,16,4,512]{3,1,2,0:T(8,128)(2,1)S(1)}, u32[]{:S(2)}, u32[]{:S(2)}) async-start(bf16[32,16,4,512]{3,1,2,0:T(8,128)(2,1)} %scatter_fusion.1), calls=%async_computation.7 | async-start | bytes 4194304 | tf_op jit(solution)/shard_map/all_to_all | solution.py:91
